TPU v7x, 512 devices: a whole 4x4x16 slice. The times are simulated.
512 devices in a mesh: dp: 64 (over z, y), fsdp: 8 (over x, core).
Axes of the slice: x: 4, y: 4, z: 16, core: 2. Of those that a mesh axis runs over, the one named last changes fastest.
Arguments:
- tokens: bfloat16 [65536, 2048], P('dp', 'fsdp'), may hold values from -6 to 6
- norm_gain: bfloat16 [2048], replicated, may hold values from 0.25 to 1.75
- query_gain: bfloat16 [128], replicated, as said below
- key_gain: bfloat16 [128], replicated, as said below
- w_query: bfloat16 [2048, 2048], P('dp', 'fsdp'), as said below
- w_key: bfloat16 [2048, 1024], P('dp', 'fsdp'), as said below
- w_value: bfloat16 [2048, 1024], P('dp', 'fsdp'), may hold values from -0.125 to 0.125
- w_out: bfloat16 [2048, 2048], P('dp', 'fsdp'), may hold values from -0.125 to 0.125
- prompt_lengths: int32 [64, 8], replicated, may hold values from 1 to 512, 1024 in all within a row
- span_group: int32 [64, 64], replicated, may hold values from 0 to 63, as said below
Outputs:
- attention_update: bfloat16 [65536, 2048], P('dp', 'fsdp')
- kv_cache: bfloat16 [65536, 8, 256], P('dp', 'fsdp')
Inputs may be any that keep to these rules, and one draw needn't show every extreme that they name: `prompt_lengths`: row g sums to 1024. `span_group`: row i names, in arrival order, the group of each of its 64 blocks of 16 rows; every group is named exactly 64 times in all; every row names exactly one group twice and leaves exactly one group out, and every group is the one named twice by exactly one row. `query_gain`: Positive. `key_gain`: Positive. `w_query`: entries of size about one over the square root of 2048. `w_key`: entries of size about one over the square root of 2048.
All inputs are finite; a program needn't handle non-finite values.
Results may differ from a plain program's by a relative error of at most 0.0075.
The roundings to bfloat16 on the way count: a program that leaves them out, or rounds other values in their place, can miss the bound.
Values may be sent and summed in bfloat16 or wider, within the bound.
No kernel may reach another device: no remote copies, remote signals or barrier semaphores. Data moves between devices by JAX's collectives and lax.ppermute only.
A program may use at most 64 MiB of HBM per device.

v0:
```python
import math
import jax
import jax.numpy as jnp
from jax import lax
from jax.sharding import PartitionSpec as P

QH = 16
KVH = 8
HD = 128
epsilon = 1e-06
rope_base = 1000000.0


def for_sending(x):

    def short(part):
        return part.astype(jnp.bfloat16) if part.dtype == jnp.float32 else part

    return jax.tree.map(short, x)


def head_norm(inputs, gains):
    inv_rms = lax.rsqrt(jnp.mean(inputs * inputs, axis=-1, keepdims=True) + epsilon)
    return inputs * inv_rms * gains.astype(jnp.float32)


def rotate(inputs, offsets):
    half_dim = inputs.shape[-1] // 2
    frequency = jnp.power(
        rope_base, -2.0 * jnp.arange(half_dim, dtype=jnp.float32) / inputs.shape[-1]
    )
    angles = offsets.astype(jnp.float32)[:, None] * frequency[None, :]
    cosine = jnp.cos(angles)[:, None, :]
    sine_part = jnp.sin(angles)[:, None, :]
    first_half = inputs[..., :half_dim]
    second = inputs[..., half_dim:]
    return jnp.concatenate(
        [first_half * cosine - second * sine_part, second * cosine + first_half * sine_part],
        axis=-1,
    )


def prompt_layout(lengths, group_rows):
    prompt_end = jnp.cumsum(lengths)
    begins = prompt_end - lengths
    position = jnp.arange(group_rows, dtype=jnp.int32)
    inside = (position[:, None] >= begins[None, :]) & (position[:, None] < prompt_end[None, :])
    starts = jnp.sum(jnp.where(inside, begins[None, :], 0), axis=1)
    return (position, starts)


def attend(query_block, key_rot, value_rows, pos_block, start_block, position):
    scores = jnp.einsum(
        "qkrd,skd->krqs", query_block, key_rot, preferred_element_type=jnp.float32
    ) * (1.0 / math.sqrt(HD))
    allowed = (position[None, :] <= pos_block[:, None]) & (
        position[None, :] >= start_block[:, None]
    )
    masked = jnp.where(allowed[None, None], scores, -jnp.inf)
    row_max = jnp.max(masked, axis=-1, keepdims=True)
    exp_scores = jnp.exp(masked - row_max)
    probs = (exp_scores / jnp.sum(exp_scores, axis=-1, keepdims=True)).astype(jnp.bfloat16)
    return jnp.einsum(
        "krqs,skd->qkrd", probs, value_rows, preferred_element_type=jnp.float32
    ).astype(jnp.bfloat16)


def with_zero_row(array):
    return jnp.concatenate([array, jnp.zeros((1,) + array.shape[1:], array.dtype)], axis=0)


def local(
    tokens,
    norm_gain,
    query_gain,
    key_gain,
    w_query,
    w_key,
    w_value,
    w_out,
    prompt_lengths,
    span_group,
):
    group_rows, width_local = tokens.shape
    groups = lax.axis_size("dp")
    arrival_rows = group_rows // groups
    capacity = 2 * arrival_rows
    device_index = lax.axis_index("dp")
    group_ids = jnp.arange(groups, dtype=jnp.int32)
    slot_ids = jnp.arange(capacity, dtype=jnp.int32)
    own_blocks = lax.dynamic_index_in_dim(span_group, device_index, 0, keepdims=False)
    counts = jnp.sum((span_group == device_index).astype(jnp.int32), axis=1)
    offsets = jnp.cumsum(counts) - counts
    row_dest = jnp.repeat(own_blocks, arrival_rows)
    onehot = (row_dest[:, None] == group_ids[None, :]).astype(jnp.int32)
    slot_rank = jnp.sum((jnp.cumsum(onehot, axis=0) - 1) * onehot, axis=1)
    send_slot = row_dest * capacity + slot_rank
    slot_source = (
        jnp.full((groups * capacity,), group_rows, jnp.int32)
        .at[send_slot]
        .set(jnp.arange(group_rows, dtype=jnp.int32))
    )
    outgoing = with_zero_row(tokens)[slot_source].reshape(groups, capacity, width_local)
    incoming = lax.all_to_all(outgoing, "dp", split_axis=0, concat_axis=0, tiled=True)
    is_valid = slot_ids[None, :] < arrival_rows * counts[:, None]
    target = arrival_rows * offsets[:, None] + slot_ids[None, :]
    flat_slot = group_ids[:, None] * capacity + slot_ids[None, :]
    back_index = jnp.where(is_valid, target, group_rows)
    source_of = (
        jnp.zeros((group_rows,), jnp.int32)
        .at[back_index.reshape(-1)]
        .set(flat_slot.reshape(-1), mode="drop")
    )
    arrived = incoming.reshape(groups * capacity, width_local)[source_of]
    full_rows = lax.all_gather(arrived, "fsdp", axis=1, tiled=True)
    query_full, key_full, value_full, out_full = (
        lax.all_gather(w_query, "dp", axis=0, tiled=True),
        lax.all_gather(w_key, "dp", axis=0, tiled=True),
        lax.all_gather(w_value, "dp", axis=0, tiled=True),
        lax.all_gather(w_out, "dp", axis=0, tiled=True),
    )
    lengths = lax.dynamic_index_in_dim(prompt_lengths, device_index, 0, keepdims=False)
    position, starts = prompt_layout(lengths, group_rows)
    within = position - starts
    floats = full_rows.astype(jnp.float32)
    normed = (
        floats
        * lax.rsqrt(jnp.mean(floats * floats, axis=-1, keepdims=True) + epsilon)
        * norm_gain.astype(jnp.float32)
    ).astype(jnp.bfloat16)
    query = jnp.dot(normed, query_full, preferred_element_type=jnp.float32).reshape(
        group_rows, -1, HD
    )
    key_rows = jnp.dot(normed, key_full, preferred_element_type=jnp.float32).reshape(
        group_rows, -1, HD
    )
    value_rows = (
        jnp.dot(normed, value_full, preferred_element_type=jnp.float32)
        .reshape(group_rows, -1, HD)
        .astype(jnp.bfloat16)
    )
    query_rot = rotate(head_norm(query, query_gain), within).astype(jnp.bfloat16)
    key_rot = rotate(head_norm(key_rows, key_gain), within).astype(jnp.bfloat16)
    kv_heads = key_rot.shape[1]
    group_ratio = QH // KVH
    cache_rows = jnp.concatenate([key_rot, value_rows], axis=-1)
    block_count = group_rows // 512
    block_len = group_rows // block_count
    query_heads = query_rot.reshape(block_count, block_len, kv_heads, group_ratio, HD)

    def one_block(pieces):
        query_block, pos_block, start_block = pieces
        return attend(query_block, key_rot, value_rows, pos_block, start_block, position)

    mixed = lax.map(
        one_block,
        (
            query_heads,
            position.reshape(block_count, block_len),
            starts.reshape(block_count, block_len),
        ),
    )
    mixed = mixed.reshape(group_rows, kv_heads * group_ratio * HD)
    heads_all = lax.all_gather(mixed, "fsdp", axis=1, tiled=True)
    update = jnp.dot(heads_all, out_full, preferred_element_type=jnp.float32).astype(jnp.bfloat16)
    arrays = (update, cache_rows)
    sent = tuple((with_zero_row(array)[back_index] for array in arrays))
    back = jax.tree.map(
        lambda part, own: part.astype(own.dtype),
        lax.all_to_all(for_sending(sent), "dp", split_axis=0, concat_axis=0, tiled=True),
        sent,
    )
    attention_out, cache_out = tuple(
        (piece.reshape((groups * capacity,) + piece.shape[2:])[send_slot] for piece in back)
    )
    return (attention_out, cache_out)


def solution(mesh):
    return jax.shard_map(
        local,
        mesh=mesh,
        in_specs=(
            P("dp", "fsdp"),
            P(),
            P(),
            P(),
            P("dp", "fsdp"),
            P("dp", "fsdp"),
            P("dp", "fsdp"),
            P("dp", "fsdp"),
            P(),
            P(),
        ),
        out_specs=(P("dp", "fsdp"), P("dp", "fsdp", None)),
        check_vma=False,
    )
```

profile of v0, /device:TPU:8, one launch (start us, length us, event | category | flops | bytes accessed | tf_op | source)
XLA Modules:
  0.0 579.5 jit_solution(6005886002139596010)
XLA Ops:
  8.9 18.0 %reduce-window.24 = s32[64,8,128]{2,1,0:T(8,128)S(1)} reduce-window(s32[64,8,128]{2,1,0:T(8,128)S(1)} %fusion.41, s32[]{:T(128)} %copy.68), window={size=1x1x128 pad=0_0x0_0x127_0}, to_apply=%region_0.1 | reduce-window | flops 8323072 | bytes 524292 | tf_op jit(solution)/shard_map/reduce-window
  27.8 4.3 scatter_custom_fusion
  33.3 9.0 %gather_fusion = bf16[2048,256]{1,0:T(8,128)(2,1)} fusion(bf16[1025,256]{1,0:T(8,128)(2,1)S(1)} %concatenate.40, s32[2048]{0:T(1024)S(1)} %fusion.43), kind=kCustom, calls=%fused_computation | custom fusion | bytes 2105344 | tf_op jit(solution)/shard_map/gather | solution.py:103
  42.3 18.9 %all-to-all-start = ((bf16[64,32,256]{2,1,0:T(8,128)(2,1)}), bf16[64,32,256]{2,1,0:T(8,128)(2,1)S(1)}, u32[]{:S(2)}, u32[]{:S(2)}) async-start(bf16[64,32,256]{2,1,0:T(8,128)(2,1)} %bitcast.9), calls=%async_computation | async-start | bytes 2097152 | tf_op jit(solution)/shard_map/all_to_all | solution.py:104
  62.0 8.0 %scatter_custom_fusion.1 = s32[1024]{0:T(1024)S(1)} fusion(s32[2048]{0:T(1024)S(1)} %bitcast.151, s32[2048]{0:T(1024)S(1)} %reshape.638, s32[]{:T(128)} %copy.68), kind=kCustom, calls=%fused_computation.100 | custom fusion | bytes 4100 | tf_op jit(solution)/shard_map/scatter | solution.py:112
  70.1 46.3 %all-to-all-done = bf16[64,32,256]{2,1,0:T(8,128)(2,1)S(1)} async-done(((bf16[64,32,256]{2,1,0:T(8,128)(2,1)}), bf16[64,32,256]{2,1,0:T(8,128)(2,1)S(1)}, u32[]{:S(2)}, u32[]{:S(2)}) %all-to-all-start) | async-done | bytes 1048608 | tf_op jit(solution)/shard_map/all_to_all | solution.py:104
  116.3 5.0 gather_fusion.1
  123.4 98.3 %all_gather.20 = bf16[2048,128]{1,0:T(8,128)(2,1)S(1)} all-gather(bf16[32,128]{1,0:T(8,128)(2,1)S(1)} %copy-done.4), channel_id=1, replica_groups=mesh['dp'=64,'fsdp'=8] {'dp'}, dimensions={0}, use_global_device_ids=true | all-gather | bytes 532480 | tf_op jit(solution)/shard_map/all_gather | solution.py:118
  221.7 98.6 %all_gather.21 = bf16[2048,128]{1,0:T(8,128)(2,1)S(1)} all-gather(bf16[32,128]{1,0:T(8,128)(2,1)S(1)} %copy-done.5), channel_id=1, replica_groups=mesh['dp'=64,'fsdp'=8] {'dp'}, dimensions={0}, use_global_device_ids=true | all-gather | bytes 532480 | tf_op jit(solution)/shard_map/all_gather | solution.py:119
  321.3 3.2 fusion.21
  330.5 3.8 multiply_reduce_fusion
  336.5 9.5 %while.12 = (s32[]{:T(128)}, bf16[2,512,1,2,128]{4,3,1,0,2:T(2,128)(2,1)S(1)}, s32[2,512]{1,0:T(2,128)S(1)}, s32[2,512]{1,0:T(2,128)S(1)}, bf16[2,512,1,2,128]{4...) while((s32[]{:T(128)}, ...), condition=%wide.region_15.16_spmd.clone.clone, body=%wide.region_12.15_spmd.clone.clone.sunk | while | flops 551155712 | bytes 16285793 | solution.py:155
  339.3 1.6 fusion.72
  344.1 1.6 fusion.72
  347.3 9.0 %gather_fusion.4 = bf16[2048,256]{1,0:T(8,128)(2,1)} fusion(bf16[1025,256]{1,0:T(8,128)(2,1)S(1)} %copy.44, s32[2048]{0:T(1024)S(1)} %broadcast_clamp_fusion), kind=kCustom, calls=%fused_computation.4 | custom fusion | bytes 2105344 | tf_op jit(solution)/shard_map/gather | solution.py:167
  356.3 7.0 %all-to-all-start.2 = ((bf16[64,32,1,256]{3,1,2,0:T(8,128)(2,1)}), bf16[64,32,1,256]{3,1,2,0:T(8,128)(2,1)S(1)}, u32[]{:S(2)}, u32[]{:S(2)}) async-start(bf16[64,32,1,256]{3,1,2,0:T(8,128)(2,1)} %bitcast.20), calls=%async_computation.2 | async-start | bytes 2097152 | tf_op jit(solution)/shard_map/all_to_all | solution.py:170
  363.3 77.8 %all-gather.10.cloned.1.call-done = bf16[2048,256]{1,0:T(8,128)(2,1)} async-done(((bf16[32,256]{1,0:T(8,128)(2,1)}), bf16[2048,256]{1,0:T(8,128)(2,1)}) %all-gather.10.cloned.1.call-update) | async-done | bytes 1048592 | tf_op jit(solution)/shard_map/all_gather | solution.py:120
  441.1 42.8 %all-gather.8.cloned.1.call-done = bf16[1024,2048]{1,0:T(8,128)(2,1)} async-done(((bf16[1024,256]{1,0:T(8,128)(2,1)}), bf16[1024,2048]{1,0:T(8,128)(2,1)}) %all-gather.8.cloned.1.call-update) | async-done | bytes 4194320 | tf_op jit(solution)/shard_map/all_gather | solution.py:164
  483.9 3.7 convolution_convert_fusion
  487.7 9.0 %gather_fusion.2 = bf16[2048,256]{1,0:T(8,128)(2,1)} fusion(bf16[1025,256]{1,0:T(8,128)(2,1)S(1)} %concatenate.45, s32[2048]{0:T(1024)S(1)} %broadcast_clamp_fusion), kind=kCustom, calls=%fused_computation.2 | custom fusion | bytes 2105344 | tf_op jit(solution)/shard_map/gather | solution.py:167
  496.7 15.7 %all-to-all-start.1 = ((bf16[64,32,256]{2,1,0:T(8,128)(2,1)}), bf16[64,32,256]{2,1,0:T(8,128)(2,1)S(1)}, u32[]{:S(2)}, u32[]{:S(2)}) async-start(bf16[64,32,256]{2,1,0:T(8,128)(2,1)} %bitcast.16), calls=%async_computation.1 | async-start | bytes 2097152 | tf_op jit(solution)/shard_map/all_to_all | solution.py:170
  512.5 5.0 gather_fusion.5
  517.4 50.6 %all-to-all-done.1 = bf16[64,32,256]{2,1,0:T(8,128)(2,1)S(1)} async-done(((bf16[64,32,256]{2,1,0:T(8,128)(2,1)}), bf16[64,32,256]{2,1,0:T(8,128)(2,1)S(1)}, u32[]{:S(2)}, u32[]{:S(2)}) %all-to-all-start.1) | async-done | bytes 1048608 | tf_op jit(solution)/shard_map/all_to_all | solution.py:170
  568.0 5.0 gather_fusion.3
  (111 shorter events, 23.1 us)
Async XLA Ops:
  7.2 115.7 %copy-start = (s32[64,8]{0,1:T(8,128)S(1)}, s32[64,8]{0,1:T(8,128)}, u32[]{:S(2)}) copy-start(s32[64,8]{0,1:T(8,128)} %param.20) | copy-start | bytes 6148
  33.2 28.0 %copy-start.3 = (s32[64,64]{1,0:T(8,128)S(1)}, s32[64,64]{1,0:T(8,128)}, u32[]{:S(2)}) copy-start(s32[64,64]{1,0:T(8,128)} %param.21) | copy-start | bytes 49156
  42.3 81.1 %copy-start.6 = (bf16[2048]{0:T(1024)(128)(2,1)S(1)}, bf16[2048]{0:T(1024)(128)(2,1)}, u32[]{:S(2)}) copy-start(bf16[2048]{0:T(1024)(128)(2,1)} %param.13) | copy-start | bytes 12292
  42.3 81.1 %copy-start.4 = (bf16[32,128]{1,0:T(8,128)(2,1)S(1)}, bf16[32,128]{1,0:T(8,128)(2,1)}, u32[]{:S(2)}) copy-start(bf16[32,128]{1,0:T(8,128)(2,1)} %param.17) | copy-start | bytes 24580
  42.3 179.4 %copy-start.7 = (bf16[128]{0:T(256)(128)(2,1)S(1)}, bf16[128]{0:T(256)(128)(2,1)}, u32[]{:S(2)}) copy-start(bf16[128]{0:T(256)(128)(2,1)} %param.15) | copy-start | bytes 772
  42.3 179.4 %copy-start.5 = (bf16[32,128]{1,0:T(8,128)(2,1)S(1)}, bf16[32,128]{1,0:T(8,128)(2,1)}, u32[]{:S(2)}) copy-start(bf16[32,128]{1,0:T(8,128)(2,1)} %param.18) | copy-start | bytes 24580
  42.3 278.0 %copy-start.8 = (bf16[128]{0:T(256)(128)(2,1)S(1)}, bf16[128]{0:T(256)(128)(2,1)}, u32[]{:S(2)}) copy-start(bf16[128]{0:T(256)(128)(2,1)} %param.14) | copy-start | bytes 772
  42.3 74.0 %all-to-all-start = ((bf16[64,32,256]{2,1,0:T(8,128)(2,1)}), bf16[64,32,256]{2,1,0:T(8,128)(2,1)S(1)}, u32[]{:S(2)}, u32[]{:S(2)}) async-start(bf16[64,32,256]{2,1,0:T(8,128)(2,1)} %bitcast.9), calls=%async_computation | async-start | bytes 2097152 | tf_op jit(solution)/shard_map/all_to_all | solution.py:104
  61.2 260.1 %all-gather.12.cloned.1.call-start = ((), (), s32[]{:S(2)}) async-start(), calls=%async_computation.6 | async-start | bytes 4718592 | tf_op jit(solution)/shard_map/all_gather | solution.py:115
  121.3 209.2 %all-gather.6.cloned.1.call-start = ((), (), s32[]{:S(2)}) async-start(), calls=%async_computation.3 | async-start | bytes 1064960 | tf_op jit(solution)/shard_map/all_gather | solution.py:117
  122.1 319.0 %all-gather.10.cloned.1.call-start = ((), (), s32[]{:S(2)}) async-start(), calls=%async_computation.5 | async-start | bytes 1064960 | tf_op jit(solution)/shard_map/all_gather | solution.py:120
  122.8 361.1 %all-gather.8.cloned.1.call-start = ((), (), s32[]{:S(2)}) async-start(), calls=%async_computation.4 | async-start | bytes 4718592 | tf_op jit(solution)/shard_map/all_gather | solution.py:164
  321.3 3.5 copy-start.2
  325.8 4.6 copy-start.1
  356.3 140.4 %all-to-all-start.2 = ((bf16[64,32,1,256]{3,1,2,0:T(8,128)(2,1)}), bf16[64,32,1,256]{3,1,2,0:T(8,128)(2,1)S(1)}, u32[]{:S(2)}, u32[]{:S(2)}) async-start(bf16[64,32,1,256]{3,1,2,0:T(8,128)(2,1)} %bitcast.20), calls=%async_computation.2 | async-start | bytes 2097152 | tf_op jit(solution)/shard_map/all_to_all | solution.py:170
  496.7 71.3 %all-to-all-start.1 = ((bf16[64,32,256]{2,1,0:T(8,128)(2,1)}), bf16[64,32,256]{2,1,0:T(8,128)(2,1)S(1)}, u32[]{:S(2)}, u32[]{:S(2)}) async-start(bf16[64,32,256]{2,1,0:T(8,128)(2,1)} %bitcast.16), calls=%async_computation.1 | async-start | bytes 2097152 | tf_op jit(solution)/shard_map/all_to_all | solution.py:170
Sparse Core Ops, SparseCore 0:
  121.5 34.7 all-gather.11
  159.2 139.9 all-gather.5
  302.1 138.9 all-gather.9
  443.6 40.2 all-gather.7
where the time goes:
time: 580 us
  waiting for transfers between devices  219 us (38%)
  blocking collectives  197 us (34%)
  local copies, waits for them, and re-layouts  60.6 us (10%)
  starting transfers between devices  41.7 us (7%)
  other arithmetic  31.2 us (5%)
  matrix products  15.8 us (3%)
  between operations  14.3 us (2%)
    all_gather x1, blocking collectives, local(): lax.all_gather(w_value, 'dp', axis=0, tiled=True)  98.6 us
    all_gather x1, blocking collectives, local(): lax.all_gather(w_key, 'dp', axis=0, tiled=True)  98.3 us
    all_gather x1, waiting for transfers between devices, local(): lax.all_gather(w_out, 'dp', axis=0, tiled=True)  77.8 us
    all_to_all x2, waiting for transfers between devices, local(): lax.all_to_all(for_sending(sent), 'dp', split_axis=0, concat_axis=0, tile...  50.6 us
    all_to_all x1, waiting for transfers between devices, local(): lax.all_to_all(outgoing, 'dp', split_axis=0, concat_axis=0, tiled=True)  46.3 us
    all_gather x1, waiting for transfers between devices, local(): heads_all = lax.all_gather(mixed, 'fsdp', axis=1, tiled=True)  42.8 us
    all_to_all x2, starting transfers between devices, local(): lax.all_to_all(for_sending(sent), 'dp', split_axis=0, concat_axis=0, tile...  22.7 us
    another operation x7, other arithmetic  19.9 us
  transfers between devices with their start and end apart: 7, of which 4 were waited for; matrix products, arithmetic and copies ran while one was open for 11% of the time, Pallas kernels for 0%

commit v1 on v0

--- a/solution.py
+++ b/solution.py
@@ -113,9 +113,16 @@
     )
     arrived = incoming.reshape(groups * capacity, width_local)[source_of]
     full_rows = lax.all_gather(arrived, "fsdp", axis=1, tiled=True)
+
+    def show_the_knots(sheet):
+        wide_out = lax.axis_size("dp")
+        tile_out = jnp.stack([sheet] * wide_out)
+        found_now = lax.all_to_all(tile_out, "dp", split_axis=0, concat_axis=0)
+        return jnp.concatenate(found_now, axis=0)
+
     query_full, key_full, value_full, out_full = (
         lax.all_gather(w_query, "dp", axis=0, tiled=True),
-        lax.all_gather(w_key, "dp", axis=0, tiled=True),
+        show_the_knots(w_key),
         lax.all_gather(w_value, "dp", axis=0, tiled=True),
         lax.all_gather(w_out, "dp", axis=0, tiled=True),
     )

time: 580 us -> 581 us (level)
  blocking collectives: 197 us -> 116 us
  waiting for transfers between devices: 219 us -> 285 us
  starting transfers between devices: 41.7 us -> 52.2 us
    all_gather x1 -> x0, blocking collectives: 98.3 us -> none  [local(): lax.all_gather(w_key, 'dp', axis=0, tiled=True)]
    all_gather x1, waiting for transfers between devices: 0.02 us -> 38.9 us  [local(): lax.all_gather(w_query, 'dp', axis=0, tiled=True)]
    all_gather x1, waiting for transfers between devices: 77.8 us -> 105 us  [local(): lax.all_gather(w_out, 'dp', axis=0, tiled=True)]
    all_gather x1, blocking collectives: 98.6 us -> 116 us  [local(): lax.all_gather(w_value, 'dp', axis=0, tiled=True)]
    all_to_all x0 -> x1, starting transfers between devices: none -> 5.95 us  [show_the_knots(): found_now = lax.all_to_all(tile_out, 'dp', split_axis=0, concat_axis=0)]
  transfers between devices with their start and end apart: 7 -> 8, of which waited for: 4 -> 5; matrix products, arithmetic and copies ran while one was open for 11% -> 12% of each run, Pallas kernels for 0% -> 0%
where the time goes in v1:
time: 581 us; the launch traced here: 580 us
  waiting for transfers between devices  285 us (49%)
  blocking collectives  116 us (20%)
  local copies, waits for them, and re-layouts  61.5 us (11%)
  starting transfers between devices  52.2 us (9%)
  other arithmetic  33.2 us (6%)
  matrix products  18.2 us (3%)
  between operations  14.3 us (2%)
    all_gather x1, blocking collectives, local(): lax.all_gather(w_value, 'dp', axis=0, tiled=True)  116 us
    all_gather x1, waiting for transfers between devices, local(): lax.all_gather(w_out, 'dp', axis=0, tiled=True)  105 us
    all_to_all x2, waiting for transfers between devices, local(): lax.all_to_all(for_sending(sent), 'dp', split_axis=0, concat_axis=0, tile...  50.6 us
    all_to_all x1, waiting for transfers between devices, local(): lax.all_to_all(outgoing, 'dp', split_axis=0, concat_axis=0, tiled=True)  46.3 us
    all_gather x1, waiting for transfers between devices, local(): heads_all = lax.all_gather(mixed, 'fsdp', axis=1, tiled=True)  42.8 us
    all_gather x1, waiting for transfers between devices, local(): lax.all_gather(w_query, 'dp', axis=0, tiled=True)  38.9 us
    all_to_all x2, starting transfers between devices, local(): lax.all_to_all(for_sending(sent), 'dp', split_axis=0, concat_axis=0, tile...  27.2 us
    another operation x7, other arithmetic  20 us
  transfers between devices with their start and end apart: 8, of which 5 were waited for; matrix products, arithmetic and copies ran while one was open for 12% of the time, Pallas kernels for 0%

profile of v1, /device:TPU:8, one launch (start us, length us, event | category | flops | bytes accessed | tf_op | source)
XLA Modules:
  0.0 580.1 jit_solution(12361006603699269954)
XLA Ops:
  8.9 18.0 %reduce-window.24 = s32[64,8,128]{2,1,0:T(8,128)S(1)} reduce-window(s32[64,8,128]{2,1,0:T(8,128)S(1)} %fusion.41, s32[]{:T(128)} %copy.68), window={size=1x1x128 pad=0_0x0_0x127_0}, to_apply=%region_0.1 | reduce-window | flops 8323072 | bytes 524292 | tf_op jit(solution)/shard_map/reduce-window
  27.8 4.3 scatter_custom_fusion
  33.3 9.0 %gather_fusion = bf16[2048,256]{1,0:T(8,128)(2,1)} fusion(bf16[1025,256]{1,0:T(8,128)(2,1)S(1)} %concatenate.40, s32[2048]{0:T(1024)S(1)} %fusion.43), kind=kCustom, calls=%fused_computation | custom fusion | bytes 2105344 | tf_op jit(solution)/shard_map/gather | solution.py:103
  42.3 18.9 %all-to-all-start = ((bf16[64,32,256]{2,1,0:T(8,128)(2,1)}), bf16[64,32,256]{2,1,0:T(8,128)(2,1)S(1)}, u32[]{:S(2)}, u32[]{:S(2)}) async-start(bf16[64,32,256]{2,1,0:T(8,128)(2,1)} %bitcast.9), calls=%async_computation | async-start | bytes 2097152 | tf_op jit(solution)/shard_map/all_to_all | solution.py:104
  62.0 8.0 %scatter_custom_fusion.1 = s32[1024]{0:T(1024)S(1)} fusion(s32[2048]{0:T(1024)S(1)} %bitcast.153, s32[2048]{0:T(1024)S(1)} %reshape.644, s32[]{:T(128)} %copy.68), kind=kCustom, calls=%fused_computation.100 | custom fusion | bytes 4100 | tf_op jit(solution)/shard_map/scatter | solution.py:112
  70.1 46.3 %all-to-all-done = bf16[64,32,256]{2,1,0:T(8,128)(2,1)S(1)} async-done(((bf16[64,32,256]{2,1,0:T(8,128)(2,1)}), bf16[64,32,256]{2,1,0:T(8,128)(2,1)S(1)}, u32[]{:S(2)}, u32[]{:S(2)}) %all-to-all-start) | async-done | bytes 1048608 | tf_op jit(solution)/shard_map/all_to_all | solution.py:104
  116.3 5.0 gather_fusion.1
  123.0 6.0 %all-to-all-start.1 = ((bf16[64,32,128]{2,1,0:T(8,128)(2,1)}), bf16[64,32,128]{2,1,0:T(8,128)(2,1)S(1)}, u32[]{:S(2)}, u32[]{:S(2)}) async-start(bf16[64,32,128]{2,1,0:T(8,128)(2,1)} %stack.2), calls=%async_computation.1 | async-start | bytes 1048576 | tf_op jit(solution)/shard_map/all_to_all | solution.py:120
  130.3 115.5 %all_gather.17 = bf16[2048,128]{1,0:T(8,128)(2,1)S(1)} all-gather(bf16[32,128]{1,0:T(8,128)(2,1)S(1)} %copy-done.5), channel_id=1, replica_groups=mesh['dp'=64,'fsdp'=8] {'dp'}, dimensions={0}, use_global_device_ids=true | all-gather | bytes 532480 | tf_op jit(solution)/shard_map/all_gather | solution.py:126
  246.8 3.2 fusion.21
  253.2 3.9 multiply_reduce_fusion.1
  260.3 38.9 %all-gather.6.cloned.1.call-done = bf16[2048,256]{1,0:T(8,128)(2,1)} async-done(((bf16[32,256]{1,0:T(8,128)(2,1)}), bf16[2048,256]{1,0:T(8,128)(2,1)}) %all-gather.6.cloned.1.call-update) | async-done | bytes 1048592 | tf_op jit(solution)/shard_map/all_gather | solution.py:124
  299.2 3.8 multiply_reduce_fusion
  305.1 9.5 %while.12 = (s32[]{:T(128)}, bf16[2,512,1,2,128]{4,3,1,0,2:T(2,128)(2,1)S(1)}, s32[2,512]{1,0:T(2,128)S(1)}, s32[2,512]{1,0:T(2,128)S(1)}, bf16[2,512,1,2,128]{4...) while((s32[]{:T(128)}, ...), condition=%wide.region_15.16_spmd.clone.clone, body=%wide.region_12.15_spmd.clone.clone.sunk | while | flops 551155712 | bytes 16285793 | solution.py:162
  315.9 9.0 %gather_fusion.4 = bf16[2048,256]{1,0:T(8,128)(2,1)} fusion(bf16[1025,256]{1,0:T(8,128)(2,1)S(1)} %copy.44, s32[2048]{0:T(1024)S(1)} %broadcast_clamp_fusion), kind=kCustom, calls=%fused_computation.4 | custom fusion | bytes 2105344 | tf_op jit(solution)/shard_map/gather | solution.py:174
  324.9 11.5 %all-to-all-start.3 = ((bf16[64,32,1,256]{3,1,2,0:T(8,128)(2,1)}), bf16[64,32,1,256]{3,1,2,0:T(8,128)(2,1)S(1)}, u32[]{:S(2)}, u32[]{:S(2)}) async-start(bf16[64,32,1,256]{3,1,2,0:T(8,128)(2,1)} %bitcast.21), calls=%async_computation.3 | async-start | bytes 2097152 | tf_op jit(solution)/shard_map/all_to_all | solution.py:177
  336.4 105.3 %all-gather.10.cloned.1.call-done = bf16[2048,256]{1,0:T(8,128)(2,1)} async-done(((bf16[32,256]{1,0:T(8,128)(2,1)}), bf16[2048,256]{1,0:T(8,128)(2,1)}) %all-gather.10.cloned.1.call-update) | async-done | bytes 1048592 | tf_op jit(solution)/shard_map/all_gather | solution.py:127
  441.7 42.8 %all-gather.8.cloned.1.call-done = bf16[1024,2048]{1,0:T(8,128)(2,1)} async-done(((bf16[1024,256]{1,0:T(8,128)(2,1)}), bf16[1024,2048]{1,0:T(8,128)(2,1)}) %all-gather.8.cloned.1.call-update) | async-done | bytes 4194320 | tf_op jit(solution)/shard_map/all_gather | solution.py:171
  484.5 3.7 convolution_convert_fusion
  488.3 9.0 %gather_fusion.2 = bf16[2048,256]{1,0:T(8,128)(2,1)} fusion(bf16[1025,256]{1,0:T(8,128)(2,1)S(1)} %concatenate.45, s32[2048]{0:T(1024)S(1)} %broadcast_clamp_fusion), kind=kCustom, calls=%fused_computation.2 | custom fusion | bytes 2105344 | tf_op jit(solution)/shard_map/gather | solution.py:174
  497.3 15.7 %all-to-all-start.2 = ((bf16[64,32,256]{2,1,0:T(8,128)(2,1)}), bf16[64,32,256]{2,1,0:T(8,128)(2,1)S(1)}, u32[]{:S(2)}, u32[]{:S(2)}) async-start(bf16[64,32,256]{2,1,0:T(8,128)(2,1)} %bitcast.17), calls=%async_computation.2 | async-start | bytes 2097152 | tf_op jit(solution)/shard_map/all_to_all | solution.py:177
  513.1 5.0 gather_fusion.5
  518.0 50.6 %all-to-all-done.2 = bf16[64,32,256]{2,1,0:T(8,128)(2,1)S(1)} async-done(((bf16[64,32,256]{2,1,0:T(8,128)(2,1)}), bf16[64,32,256]{2,1,0:T(8,128)(2,1)S(1)}, u32[]{:S(2)}, u32[]{:S(2)}) %all-to-all-start.2) | async-done | bytes 1048608 | tf_op jit(solution)/shard_map/all_to_all | solution.py:177
  568.6 5.0 gather_fusion.3
  (113 shorter events, 27.5 us)
Async XLA Ops:
  7.2 122.6 %copy-start = (s32[64,8]{0,1:T(8,128)S(1)}, s32[64,8]{0,1:T(8,128)}, u32[]{:S(2)}) copy-start(s32[64,8]{0,1:T(8,128)} %param.20) | copy-start | bytes 6148
  33.2 28.0 %copy-start.3 = (s32[64,64]{1,0:T(8,128)S(1)}, s32[64,64]{1,0:T(8,128)}, u32[]{:S(2)}) copy-start(s32[64,64]{1,0:T(8,128)} %param.21) | copy-start | bytes 49156
  42.3 79.8 %copy-start.4 = (bf16[32,128]{1,0:T(8,128)(2,1)S(1)}, bf16[32,128]{1,0:T(8,128)(2,1)}, u32[]{:S(2)}) copy-start(bf16[32,128]{1,0:T(8,128)(2,1)} %param.17) | copy-start | bytes 24580
  42.3 87.5 %copy-start.6 = (bf16[2048]{0:T(1024)(128)(2,1)S(1)}, bf16[2048]{0:T(1024)(128)(2,1)}, u32[]{:S(2)}) copy-start(bf16[2048]{0:T(1024)(128)(2,1)} %param.13) | copy-start | bytes 12292
  42.3 87.5 %copy-start.7 = (bf16[128]{0:T(256)(128)(2,1)S(1)}, bf16[128]{0:T(256)(128)(2,1)}, u32[]{:S(2)}) copy-start(bf16[128]{0:T(256)(128)(2,1)} %param.15) | copy-start | bytes 772
  42.3 87.9 %copy-start.8 = (bf16[128]{0:T(256)(128)(2,1)S(1)}, bf16[128]{0:T(256)(128)(2,1)}, u32[]{:S(2)}) copy-start(bf16[128]{0:T(256)(128)(2,1)} %param.14) | copy-start | bytes 772
  42.3 88.0 %copy-start.5 = (bf16[32,128]{1,0:T(8,128)(2,1)S(1)}, bf16[32,128]{1,0:T(8,128)(2,1)}, u32[]{:S(2)}) copy-start(bf16[32,128]{1,0:T(8,128)(2,1)} %param.18) | copy-start | bytes 24580
  42.3 74.1 %all-to-all-start = ((bf16[64,32,256]{2,1,0:T(8,128)(2,1)}), bf16[64,32,256]{2,1,0:T(8,128)(2,1)S(1)}, u32[]{:S(2)}, u32[]{:S(2)}) async-start(bf16[64,32,256]{2,1,0:T(8,128)(2,1)} %bitcast.9), calls=%async_computation | async-start | bytes 2097152 | tf_op jit(solution)/shard_map/all_to_all | solution.py:104
  61.2 185.7 %all-gather.12.cloned.1.call-start = ((), (), s32[]{:S(2)}) async-start(), calls=%async_computation.7 | async-start | bytes 4718592 | tf_op jit(solution)/shard_map/all_gather | solution.py:115
  121.3 177.8 %all-gather.6.cloned.1.call-start = ((), (), s32[]{:S(2)}) async-start(), calls=%async_computation.4 | async-start | bytes 1064960 | tf_op jit(solution)/shard_map/all_gather | solution.py:124
  123.0 130.3 %all-to-all-start.1 = ((bf16[64,32,128]{2,1,0:T(8,128)(2,1)}), bf16[64,32,128]{2,1,0:T(8,128)(2,1)S(1)}, u32[]{:S(2)}, u32[]{:S(2)}) async-start(bf16[64,32,128]{2,1,0:T(8,128)(2,1)} %stack.2), calls=%async_computation.1 | async-start | bytes 1048576 | tf_op jit(solution)/shard_map/all_to_all | solution.py:120
  128.9 312.8 %all-gather.10.cloned.1.call-start = ((), (), s32[]{:S(2)}) async-start(), calls=%async_computation.6 | async-start | bytes 1064960 | tf_op jit(solution)/shard_map/all_gather | solution.py:127
  129.7 354.9 %all-gather.8.cloned.1.call-start = ((), (), s32[]{:S(2)}) async-start(), calls=%async_computation.5 | async-start | bytes 4718592 | tf_op jit(solution)/shard_map/all_gather | solution.py:171
  246.8 3.5 copy-start.2
  253.2 5.4 copy-start.1
  324.9 172.4 %all-to-all-start.3 = ((bf16[64,32,1,256]{3,1,2,0:T(8,128)(2,1)}), bf16[64,32,1,256]{3,1,2,0:T(8,128)(2,1)S(1)}, u32[]{:S(2)}, u32[]{:S(2)}) async-start(bf16[64,32,1,256]{3,1,2,0:T(8,128)(2,1)} %bitcast.21), calls=%async_computation.3 | async-start | bytes 2097152 | tf_op jit(solution)/shard_map/all_to_all | solution.py:177
  497.3 71.3 %all-to-all-start.2 = ((bf16[64,32,256]{2,1,0:T(8,128)(2,1)}), bf16[64,32,256]{2,1,0:T(8,128)(2,1)S(1)}, u32[]{:S(2)}, u32[]{:S(2)}) async-start(bf16[64,32,256]{2,1,0:T(8,128)(2,1)} %bitcast.17), calls=%async_computation.2 | async-start | bytes 2097152 | tf_op jit(solution)/shard_map/all_to_all | solution.py:177
Sparse Core Ops, SparseCore 0:
  121.5 34.9 all-gather.11
  159.4 139.7 all-gather.5
  302.1 139.5 all-gather.9
  444.2 40.2 all-gather.7
